TPU v7x, 512 devices: a whole 4x8x8 slice. The times are simulated.
512 devices in a mesh: tm: 32 (over y, x), rows: 16 (over z, core).
Axes of the slice: x: 4, y: 8, z: 8, core: 2. Of those that a mesh axis runs over, the one named last changes fastest.
Arguments:
- features: bfloat16 [64, 16, 40, 384], P('tm', 'rows'), may hold values from -6 to 6
- gain_one: float32 [384], replicated, may hold values from 0.1 to 1.9
- weight_one: bfloat16 [384, 3, 3, 3, 384], P('rows'), may hold values from -0.0625 to 0.0625
- bias_one: float32 [384], replicated, may hold values from -3 to 3
- gain_two: float32 [384], replicated, may hold values from 0.1 to 1.9
- weight_two: bfloat16 [384, 3, 3, 3, 384], P('rows'), may hold values from -0.0625 to 0.0625
- bias_two: float32 [384], replicated, may hold values from -3 to 3
Outputs:
- block_out: bfloat16 [64, 16, 40, 384], P('tm', 'rows')
All inputs are finite; a program needn't handle non-finite values.
Results may differ from a plain program's by a relative error of at most 0.0049.
Values may be sent and summed in bfloat16 or wider, within the bound.
No kernel may reach another device: no remote copies, remote signals or barrier semaphores. Data moves between devices by JAX's collectives and lax.ppermute only.
A program may use at most 64 MiB of HBM per device.

v0:
```python
import jax
import jax.numpy as jnp
from jax import lax
from jax.sharding import PartitionSpec as P


def passed_along(x, axis, by):
    peers = lax.axis_size(axis)
    pairs = [(i, i + by) for i in range(peers) if 0 <= i + by < peers]
    return lax.ppermute(x, axis, pairs)


def norm_silu(values, norm_gain):
    values = values.astype(jnp.float32)
    mean_square = jnp.mean(values * values, axis=-1, keepdims=True)
    scaled = values * lax.rsqrt(mean_square + 1e-06) * norm_gain
    return jax.nn.silu(scaled).astype(jnp.bfloat16)


def causal_conv(extended, kernel, bias_part):
    frames = extended.shape[0] - 2
    height = extended.shape[1]
    columns = extended.shape[2]
    channels = extended.shape[3]
    part_width = kernel.shape[0]
    folded = 9 * part_width
    padded_width = (folded + 127) // 128 * 128
    padded = jnp.pad(extended, ((0, 0), (1, 1), (1, 1), (0, 0)))
    summed = jnp.zeros((frames, height, columns, part_width), jnp.float32)
    for tap_time in range(3):
        slab = padded[tap_time : tap_time + frames]
        taps = jnp.transpose(kernel[:, tap_time], (1, 2, 0, 3)).reshape(folded, channels)
        taps = jnp.pad(taps, ((0, padded_width - folded), (0, 0)))
        product = lax.dot_general(
            slab.reshape(-1, channels),
            taps,
            (((1,), (1,)), ((), ())),
            preferred_element_type=jnp.float32,
        )
        product = product[:, :folded].reshape(frames, height + 2, columns + 2, 3, 3, part_width)
        for tap_row in range(3):
            for tap_col in range(3):
                summed = (
                    summed
                    + product[
                        :, tap_row : tap_row + height, tap_col : tap_col + columns, tap_row, tap_col
                    ]
                )
    return summed + bias_part


def shards(features, gain_one, weight_one, bias_one, gain_two, weight_two, bias_two):
    part_width = weight_one.shape[0]
    offset = lax.axis_index("rows") * part_width
    bias_first = lax.dynamic_slice_in_dim(bias_one, offset, part_width, 0)
    bias_second = lax.dynamic_slice_in_dim(bias_two, offset, part_width, 0)
    normed_one = norm_silu(features, gain_one)
    prior_one = passed_along(normed_one, "tm", 1)
    extended_one = jnp.concatenate([prior_one, normed_one], 0)
    full_one = lax.all_gather(extended_one, "rows", axis=1, tiled=True)
    conv_one = causal_conv(full_one, weight_one, bias_first).astype(jnp.bfloat16)
    own_rows = lax.all_to_all(conv_one, "rows", split_axis=1, concat_axis=3, tiled=True)
    normed_two = norm_silu(own_rows, gain_two)
    prior_two = passed_along(normed_two, "tm", 1)
    extended_two = jnp.concatenate([prior_two, normed_two], 0)
    full_two = lax.all_gather(extended_two, "rows", axis=1, tiled=True)
    conv_two = causal_conv(full_two, weight_two, bias_second)
    returned = lax.all_to_all(conv_two, "rows", split_axis=1, concat_axis=3, tiled=True)
    return (features.astype(jnp.float32) + returned).astype(jnp.bfloat16)


def solution(mesh):
    in_specs = (
        P("tm", "rows", None, None),
        P(),
        P("rows", None, None, None, None),
        P(),
        P(),
        P("rows", None, None, None, None),
        P(),
    )
    out_specs = P("tm", "rows", None, None)
    return jax.shard_map(shards, mesh=mesh, in_specs=in_specs, out_specs=out_specs, check_vma=False)
```

profile of v0, /device:TPU:1, one launch (start us, length us, event | category | flops | bytes accessed | tf_op | source)
XLA Modules:
  0.0 217.8 jit_solution(14636832090744077345)
XLA Ops:
  6.5 0.9 fusion.25
  7.5 0.9 fusion.32
  8.4 3.9 %collective-permute-start = (bf16[2,1,40,384]{3,2,1,0:T(8,128)(2,1)S(1)}, bf16[2,1,40,384]{3,2,1,0:T(8,128)(2,1)S(1)}, u32[]{:S(2)}, u32[]{:S(2)}) collective-permute-start(bf16[2,1,40,384]{3,2,1,0:T(8,128)(2,1)S(1)} %fusion.32), channel_id=1, source_target_pairs={{0,16},{16,32},{32,48},{48,64},{64,80},{80,96},{96,112},{112,128},... | collective-permute-start | bytes 184328 | tf_op jit(solution)/shard_map/ppermute | solution.py:10
  12.4 1.3 collective-permute-done
  13.7 0.7 maximum_bitcast_fusion
  14.4 0.8 dynamic_slice.6
  15.2 1.1 fusion.35
  16.3 48.9 %all-gather.3.cloned.1.call-done = bf16[4,16,40,384]{3,2,0,1:T(8,128)(2,1)} async-done(((bf16[4,1,40,384]{3,2,0,1:T(8,128)(2,1)}), bf16[4,16,40,384]{3,2,0,1:T(8,128)(2,1)}) %all-gather.3.cloned.1.call-update) | async-done | bytes 1966096 | tf_op jit(solution)/shard_map/all_gather | solution.py:60
  65.2 4.8 %pad_slice_fusion.5 = (bf16[2,18,42,384]{3,2,0,1:T(8,128)(2,1)S(1)}, bf16[2,18,42,384]{3,2,0,1:T(8,128)(2,1)}, bf16[2,18,42,384]{3,2,0,1:T(8,128)(2,1)S(1)}) fusion(bf16[4,16,40,384]{3,2,0,1:T(8,128)(2,1)} %all-gather.3.cloned.1.call-done), kind=kLoop, calls=%fused_computation.5 | loop fusion | bytes 5449728 | tf_op jit(solution)/shard_map/slice | solution.py:31
  70.2 1.3 reshape.154
  71.5 1.9 fusion.38
  73.4 4.3 %reshape.156 = f32[2,18,42,3,3,24]{2,1,0,5,4,3:T(8,128)} reshape(f32[1512,216]{0,1:T(8,128)S(1)} %fusion.38) | data formatting | bytes 2612736 | tf_op jit(solution)/shard_map/reshape | solution.py:40
  77.7 1.5 copy.58
  79.2 1.4 reshape.151
  80.5 1.9 fusion.37
  82.4 4.4 %reshape.153 = f32[2,18,42,3,3,24]{2,1,0,5,4,3:T(8,128)} reshape(f32[1512,216]{0,1:T(8,128)S(1)} %fusion.37) | data formatting | bytes 2612736 | tf_op jit(solution)/shard_map/reshape | solution.py:40
  86.9 0.3 reshape.148
  87.3 0.6 fusion.36
  87.9 4.3 %reshape.150 = f32[2,18,42,3,3,24]{2,1,0,5,4,3:T(8,128)} reshape(f32[1512,216]{0,1:T(8,128)S(1)} %fusion.36) | data formatting | bytes 2612736 | tf_op jit(solution)/shard_map/reshape | solution.py:40
  92.2 7.0 %fusion.14 = bf16[2,16,40,24]{2,1,0,3:T(8,128)(2,1)S(1)} fusion(f32[2,18,42,3,3,24]{2,1,0,5,4,3:T(8,128)} %reshape.156, f32[2,18,42,3,3,24]{2,1,0,5,4,3:T(8,128)} %reshape.153, f32[2,18,42,3,3,24]{2,1,0,5,4,3:T(8,128)} %reshape.150, f32[24]{0:T(128)S(1)} %dynamic_slice.6), kind=kLoop, calls=%fused_computation.47 | loop fusion | flops 860160 | bytes 3379296 | tf_op jit(solution)/shard_map/convert_element_type | solution.py:61
  99.3 0.2 reshape.192
  99.6 12.0 %all_to_all.27 = bf16[16,2,960]{2,1,0:T(2,128)(2,1)S(1)} all-to-all(bf16[16,2,960]{2,1,0:T(2,128)(2,1)S(1)} %reshape.192), channel_id=1, replica_groups=mesh['tm'=32,'rows'=16] {'rows'}, dimensions={0} | all-to-all | bytes 122880 | tf_op jit(solution)/shard_map/all_to_all | solution.py:62
  111.6 0.2 reshape.193
  112.0 0.4 multiply_reduce_fusion
  112.7 3.3 %collective-permute-start.1 = (bf16[2,1,40,384]{3,2,1,0:T(8,128)(2,1)S(1)}, bf16[2,1,40,384]{3,2,1,0:T(8,128)(2,1)S(1)}, u32[]{:S(2)}, u32[]{:S(2)}) collective-permute-start(bf16[2,1,40,384]{3,2,1,0:T(8,128)(2,1)S(1)} %multiply_convert_fusion), channel_id=1, source_target_pairs={{0,16},{16,32},{32,48},{48,64},{64,80},{80,96},{96,112},{112,128},... | collective-permute-start | bytes 184328 | tf_op jit(solution)/shard_map/ppermute | solution.py:10
  116.0 1.1 collective-permute-done.1
  117.1 0.7 maximum_bitcast_fusion.1
  117.8 0.8 dynamic_slice.7
  118.6 41.3 %all-gather.5.cloned.1.call-done = bf16[4,16,40,384]{3,2,0,1:T(8,128)(2,1)} async-done(((bf16[4,1,40,384]{3,2,0,1:T(8,128)(2,1)}), bf16[4,16,40,384]{3,2,0,1:T(8,128)(2,1)}) %all-gather.5.cloned.1.call-update) | async-done | bytes 1966096 | tf_op jit(solution)/shard_map/all_gather | solution.py:66
  159.9 4.8 %pad_slice_fusion.2 = (bf16[2,18,42,384]{3,2,0,1:T(8,128)(2,1)S(1)}, bf16[2,18,42,384]{3,2,0,1:T(8,128)(2,1)}, bf16[2,18,42,384]{3,2,0,1:T(8,128)(2,1)S(1)}) fusion(bf16[4,16,40,384]{3,2,0,1:T(8,128)(2,1)} %all-gather.5.cloned.1.call-done), kind=kLoop, calls=%fused_computation.2 | loop fusion | bytes 5449728 | tf_op jit(solution)/shard_map/slice | solution.py:31
  164.8 1.3 reshape.163
  166.1 1.9 fusion.41
  168.0 4.3 %reshape.165 = f32[2,18,42,3,3,24]{2,1,0,5,4,3:T(8,128)} reshape(f32[1512,216]{0,1:T(8,128)S(1)} %fusion.41) | data formatting | bytes 2612736 | tf_op jit(solution)/shard_map/reshape | solution.py:40
  172.4 1.5 copy.65
  173.8 1.4 reshape.160
  175.2 1.9 fusion.40
  177.1 4.4 %reshape.162 = f32[2,18,42,3,3,24]{2,1,0,5,4,3:T(8,128)} reshape(f32[1512,216]{0,1:T(8,128)S(1)} %fusion.40) | data formatting | bytes 2612736 | tf_op jit(solution)/shard_map/reshape | solution.py:40
  181.6 0.3 reshape.157
  181.9 0.6 fusion.39
  182.5 4.3 %reshape.159 = f32[2,18,42,3,3,24]{2,1,0,5,4,3:T(8,128)} reshape(f32[1512,216]{0,1:T(8,128)S(1)} %fusion.39) | data formatting | bytes 2612736 | tf_op jit(solution)/shard_map/reshape | solution.py:40
  186.8 7.0 %fusion.1 = f32[2,16,40,24]{2,1,0,3:T(8,128)S(1)} fusion(f32[2,18,42,3,3,24]{2,1,0,5,4,3:T(8,128)} %reshape.165, f32[2,18,42,3,3,24]{2,1,0,5,4,3:T(8,128)} %reshape.162, f32[2,18,42,3,3,24]{2,1,0,5,4,3:T(8,128)} %reshape.159, f32[24]{0:T(128)S(1)} %dynamic_slice.7), kind=kLoop, calls=%fused_computation.8 | loop fusion | flops 829440 | bytes 3440736 | tf_op jit(solution)/shard_map/add | solution.py:49
  193.8 0.2 copy.76
  194.0 0.7 reshape.194
  194.8 13.2 %all_to_all.28 = f32[16,1,1920]{2,1,0:T(1,128)S(1)} all-to-all(f32[16,1,1920]{2,1,0:T(1,128)S(1)} %reshape.194), channel_id=1, replica_groups=mesh['tm'=32,'rows'=16] {'rows'}, dimensions={0} | all-to-all | bytes 245760 | tf_op jit(solution)/shard_map/all_to_all | solution.py:68
  208.0 0.5 broadcast.93
  208.5 0.9 reduce.5
  209.4 0.7 reshape.195
  210.3 0.6 fusion.33
  (22 shorter events, 1.4 us)
Async XLA Ops:
  6.5 58.7 %all-gather.3.cloned.1.call-start = ((), (), s32[]{:S(2)}) async-start(), calls=%async_computation.2 | async-start | bytes 2088960 | tf_op jit(solution)/shard_map/all_gather | solution.py:60
  8.4 5.2 %collective-permute-start = (bf16[2,1,40,384]{3,2,1,0:T(8,128)(2,1)S(1)}, bf16[2,1,40,384]{3,2,1,0:T(8,128)(2,1)S(1)}, u32[]{:S(2)}, u32[]{:S(2)}) collective-permute-start(bf16[2,1,40,384]{3,2,1,0:T(8,128)(2,1)S(1)} %fusion.32), channel_id=1, source_target_pairs={{0,16},{16,32},{32,48},{48,64},{64,80},{80,96},{96,112},{112,128},... | collective-permute-start | bytes 184328 | tf_op jit(solution)/shard_map/ppermute | solution.py:10
  14.3 145.5 %all-gather.5.cloned.1.call-start = ((), (), s32[]{:S(2)}) async-start(), calls=%async_computation.3 | async-start | bytes 2088960 | tf_op jit(solution)/shard_map/all_gather | solution.py:66
  99.2 13.4 %copy-start.2 = (f32[384]{0:T(512)S(1)}, f32[384]{0:T(512)}, u32[]{:S(2)}) copy-start(f32[384]{0:T(512)} %param.11) | copy-start | bytes 4612
  99.3 19.2 %copy-start.1 = (bf16[24,3,3,3,384]{4,0,3,2,1:T(8,128)(2,1)S(1)}, bf16[24,3,3,3,384]{4,0,3,2,1:T(8,128)(2,1)}, u32[]{:S(2)}) copy-start(bf16[24,3,3,3,384]{4,0,3,2,1:T(8,128)(2,1)} %param.12) | copy-start | bytes 1492996
  112.7 4.4 %collective-permute-start.1 = (bf16[2,1,40,384]{3,2,1,0:T(8,128)(2,1)S(1)}, bf16[2,1,40,384]{3,2,1,0:T(8,128)(2,1)S(1)}, u32[]{:S(2)}, u32[]{:S(2)}) collective-permute-start(bf16[2,1,40,384]{3,2,1,0:T(8,128)(2,1)S(1)} %multiply_convert_fusion), channel_id=1, source_target_pairs={{0,16},{16,32},{32,48},{48,64},{64,80},{80,96},{96,112},{112,128},... | collective-permute-start | bytes 184328 | tf_op jit(solution)/shard_map/ppermute | solution.py:10
  193.8 16.5 %copy-start = (bf16[2,1,40,384]{3,2,1,0:T(8,128)(2,1)S(1)}, bf16[2,1,40,384]{3,2,1,0:T(8,128)(2,1)}, u32[]{:S(2)}) copy-start(bf16[2,1,40,384]{3,2,1,0:T(8,128)(2,1)} %param.7) | copy-start | bytes 184324
Sparse Core Ops, SparseCore 0:
  14.5 50.7 all-gather.2
  117.9 41.9 all-gather.4
where the time goes:
time: 218 us
  waiting for transfers between devices  92.6 us (42%)
  local copies, waits for them, and re-layouts  50.8 us (23%)
  blocking collectives  25.2 us (12%)
  other arithmetic  19.4 us (9%)
  between operations  13.6 us (6%)
  matrix products  8.8 us (4%)
  starting transfers between devices  7.28 us (3%)
    all_gather x1, waiting for transfers between devices, shards(): full_one = lax.all_gather(extended_one, 'rows', axis=1, tiled=True)  48.9 us
    all_gather x1, waiting for transfers between devices, shards(): full_two = lax.all_gather(extended_two, 'rows', axis=1, tiled=True)  41.3 us
    reshape x6, local copies, waits for them, and re-layouts, causal_conv(): product[:, :folded]  25.9 us
    all_to_all x1, blocking collectives, shards(): lax.all_to_all(conv_two, 'rows', split_axis=1, concat_axis=3, tiled=True)  13.2 us
    slice x8, local copies, waits for them, and re-layouts, causal_conv(): slab = padded[tap_time:tap_time + frames]  13.1 us
    all_to_all x1, blocking collectives, shards(): lax.all_to_all(conv_one, 'rows', split_axis=1, concat_axis=3, tiled=True)  12 us
    dot_general x6, matrix products, causal_conv(): lax.dot_general(slab.reshape(-1, channels), taps, (((1,), (1,)), ((), ())...  8.8 us
    ppermute x2, starting transfers between devices, passed_along(): return lax.ppermute(x, axis, pairs)  7.24 us
  transfers between devices with their start and end apart: 4, of which 4 were waited for; matrix products, arithmetic and copies ran while one was open for 1% of the time, Pallas kernels for 0%

commit v1 on v0

--- a/solution.py
+++ b/solution.py
@@ -2,6 +2,7 @@
 import jax.numpy as jnp
 from jax import lax
 from jax.sharding import PartitionSpec as P
+from jax.lax import all_to_all, axis_size
 
 
 def passed_along(x, axis, by):
@@ -63,7 +64,9 @@
     normed_two = norm_silu(own_rows, gain_two)
     prior_two = passed_along(normed_two, "tm", 1)
     extended_two = jnp.concatenate([prior_two, normed_two], 0)
-    full_two = lax.all_gather(extended_two, "rows", axis=1, tiled=True)
+    full_two = jnp.concatenate(
+        all_to_all(jnp.stack([extended_two] * axis_size("rows"), 0), "rows", 0, 0), axis=1
+    )
     conv_two = causal_conv(full_two, weight_two, bias_second)
     returned = lax.all_to_all(conv_two, "rows", split_axis=1, concat_axis=3, tiled=True)
     return (features.astype(jnp.float32) + returned).astype(jnp.bfloat16)

time: 218 us -> 229 us (1.050); the launches traced: 218 us -> 225 us
  starting transfers between devices: 7.28 us -> 11.7 us
  waiting for transfers between devices: 92.6 us -> 96.4 us
    all_to_all x0 -> x1, waiting for transfers between devices: none -> 44.8 us  [shards(): all_to_all(jnp.stack([extended_two] * axis_size('rows'), 0), 'rows', 0, 0)]
    all_gather x1 -> x0, waiting for transfers between devices: 41.3 us -> none  [shards(): full_two = lax.all_gather(extended_two, 'rows', axis=1, tiled=True)]
    all_to_all x0 -> x1, starting transfers between devices: none -> 4.65 us  [shards(): all_to_all(jnp.stack([extended_two] * axis_size('rows'), 0), 'rows', 0, 0)]
    slice x8, local copies, waits for them, and re-layouts: 13.1 us -> 10.6 us  [causal_conv(): slab = padded[tap_time:tap_time + frames]]
  transfers between devices with their start and end apart: 4 -> 4, of which waited for: 4 -> 4; matrix products, arithmetic and copies ran while one was open for 1% -> 2% of each run, Pallas kernels for 0% -> 0%
where the time goes in v1:
time: 229 us; the launch traced here: 225 us
  waiting for transfers between devices  96.4 us (42%)
  local copies, waits for them, and re-layouts  50.5 us (22%)
  blocking collectives  25.6 us (11%)
  other arithmetic  18.8 us (8%)
  between operations  13.6 us (6%)
  starting transfers between devices  11.7 us (5%)
  matrix products  8.78 us (4%)
    all_gather x1, waiting for transfers between devices, shards(): full_one = lax.all_gather(extended_one, 'rows', axis=1, tiled=True)  49 us
    all_to_all x1, waiting for transfers between devices, shards(): all_to_all(jnp.stack([extended_two] * axis_size('rows'), 0), 'rows', 0, 0)  44.8 us
    reshape x6, local copies, waits for them, and re-layouts, causal_conv(): product[:, :folded]  25.9 us
    all_to_all x1, blocking collectives, shards(): lax.all_to_all(conv_two, 'rows', split_axis=1, concat_axis=3, tiled=True)  13.6 us
    all_to_all x1, blocking collectives, shards(): lax.all_to_all(conv_one, 'rows', split_axis=1, concat_axis=3, tiled=True)  12 us
    slice x8, local copies, waits for them, and re-layouts, causal_conv(): slab = padded[tap_time:tap_time + frames]  10.6 us
    dot_general x6, matrix products, causal_conv(): lax.dot_general(slab.reshape(-1, channels), taps, (((1,), (1,)), ((), ())...  8.78 us
    ppermute x2, starting transfers between devices, passed_along(): return lax.ppermute(x, axis, pairs)  7.03 us
  transfers between devices with their start and end apart: 4, of which 4 were waited for; matrix products, arithmetic and copies ran while one was open for 2% of the time, Pallas kernels for 0%

profile of v1, /device:TPU:1, one launch (start us, length us, event | category | flops | bytes accessed | tf_op | source)
XLA Modules:
  0.0 225.4 jit_solution(14026688927869705534)
XLA Ops:
  6.5 0.9 fusion.25
  7.5 0.9 fusion.32
  8.4 3.9 %collective-permute-start = (bf16[2,1,40,384]{3,2,1,0:T(8,128)(2,1)S(1)}, bf16[2,1,40,384]{3,2,1,0:T(8,128)(2,1)S(1)}, u32[]{:S(2)}, u32[]{:S(2)}) collective-permute-start(bf16[2,1,40,384]{3,2,1,0:T(8,128)(2,1)S(1)} %fusion.32), channel_id=1, source_target_pairs={{0,16},{16,32},{32,48},{48,64},{64,80},{80,96},{96,112},{112,128},... | collective-permute-start | bytes 184328 | tf_op jit(solution)/shard_map/ppermute | solution.py:11
  12.4 1.3 collective-permute-done
  13.7 0.7 maximum_bitcast_fusion
  14.3 0.8 dynamic_slice.6
  15.1 1.1 fusion.35
  16.2 49.0 %all-gather.2.cloned.1.call-done = bf16[4,16,40,384]{3,2,0,1:T(8,128)(2,1)} async-done(((bf16[4,1,40,384]{3,2,0,1:T(8,128)(2,1)}), bf16[4,16,40,384]{3,2,0,1:T(8,128)(2,1)}) %all-gather.2.cloned.1.call-update) | async-done | bytes 1966096 | tf_op jit(solution)/shard_map/all_gather | solution.py:61
  65.2 4.8 %pad_slice_fusion.5 = (bf16[2,18,42,384]{3,2,0,1:T(8,128)(2,1)S(1)}, bf16[2,18,42,384]{3,2,0,1:T(8,128)(2,1)}, bf16[2,18,42,384]{3,2,0,1:T(8,128)(2,1)S(1)}) fusion(bf16[4,16,40,384]{3,2,0,1:T(8,128)(2,1)} %all-gather.2.cloned.1.call-done), kind=kLoop, calls=%fused_computation.5 | loop fusion | bytes 5449728 | tf_op jit(solution)/shard_map/slice | solution.py:32
  70.2 1.3 reshape.163
  71.5 1.9 fusion.38
  73.4 4.3 %reshape.165 = f32[2,18,42,3,3,24]{2,1,0,5,4,3:T(8,128)} reshape(f32[1512,216]{0,1:T(8,128)S(1)} %fusion.38) | data formatting | bytes 2612736 | tf_op jit(solution)/shard_map/reshape | solution.py:41
  77.7 1.5 copy.57
  79.2 1.4 reshape.160
  80.6 1.9 fusion.37
  82.4 4.4 %reshape.162 = f32[2,18,42,3,3,24]{2,1,0,5,4,3:T(8,128)} reshape(f32[1512,216]{0,1:T(8,128)S(1)} %fusion.37) | data formatting | bytes 2612736 | tf_op jit(solution)/shard_map/reshape | solution.py:41
  86.9 0.3 reshape.157
  87.3 0.6 fusion.36
  87.9 4.3 %reshape.159 = f32[2,18,42,3,3,24]{2,1,0,5,4,3:T(8,128)} reshape(f32[1512,216]{0,1:T(8,128)S(1)} %fusion.36) | data formatting | bytes 2612736 | tf_op jit(solution)/shard_map/reshape | solution.py:41
  92.2 7.0 %fusion.14 = bf16[2,16,40,24]{2,1,0,3:T(8,128)(2,1)S(1)} fusion(f32[2,18,42,3,3,24]{2,1,0,5,4,3:T(8,128)} %reshape.165, f32[2,18,42,3,3,24]{2,1,0,5,4,3:T(8,128)} %reshape.162, f32[2,18,42,3,3,24]{2,1,0,5,4,3:T(8,128)} %reshape.159, f32[24]{0:T(128)S(1)} %dynamic_slice.6), kind=kLoop, calls=%fused_computation.47 | loop fusion | flops 860160 | bytes 3379296 | tf_op jit(solution)/shard_map/convert_element_type | solution.py:62
  99.3 0.2 reshape.203
  99.6 12.0 %all_to_all.32 = bf16[16,2,960]{2,1,0:T(2,128)(2,1)S(1)} all-to-all(bf16[16,2,960]{2,1,0:T(2,128)(2,1)S(1)} %reshape.203), channel_id=1, replica_groups=mesh['tm'=32,'rows'=16] {'rows'}, dimensions={0} | all-to-all | bytes 122880 | tf_op jit(solution)/shard_map/all_to_all | solution.py:63
  112.0 0.4 multiply_reduce_fusion
  112.7 3.1 %collective-permute-start.1 = (bf16[2,1,40,384]{3,2,1,0:T(8,128)(2,1)S(1)}, bf16[2,1,40,384]{3,2,1,0:T(8,128)(2,1)S(1)}, u32[]{:S(2)}, u32[]{:S(2)}) collective-permute-start(bf16[2,1,40,384]{3,2,1,0:T(8,128)(2,1)S(1)} %multiply_convert_fusion), channel_id=1, source_target_pairs={{0,16},{16,32},{32,48},{48,64},{64,80},{80,96},{96,112},{112,128},... | collective-permute-start | bytes 184328 | tf_op jit(solution)/shard_map/ppermute | solution.py:11
  115.8 1.3 collective-permute-done.1
  117.1 1.5 stack.2
  118.6 4.7 %all-to-all-start.1 = ((bf16[16,4,1,40,384]{4,3,1,2,0:T(8,128)(2,1)}), bf16[16,4,1,40,384]{4,3,1,2,0:T(8,128)(2,1)S(1)}, u32[]{:S(2)}, u32[]{:S(2)}) async-start(bf16[16,4,1,40,384]{4,3,1,2,0:T(8,128)(2,1)} %stack.2), calls=%async_computation.1 | async-start | bytes 3932160 | tf_op jit(solution)/shard_map/all_to_all | solution.py:68
  123.2 0.8 dynamic_slice.7
  124.0 0.8 fusion.34
  124.8 44.8 %all-to-all-done.1 = bf16[16,4,1,40,384]{4,3,1,2,0:T(8,128)(2,1)S(1)} async-done(((bf16[16,4,1,40,384]{4,3,1,2,0:T(8,128)(2,1)}), bf16[16,4,1,40,384]{4,3,1,2,0:T(8,128)(2,1)S(1)}, u32[]{:S(2)}, u32[]{:S(2)}) %all-to-all-start.1) | async-done | bytes 1966112 | tf_op jit(solution)/shard_map/all_to_all | solution.py:68
  169.6 2.3 %pad_slice_fusion.2 = (bf16[2,18,42,384]{3,2,0,1:T(8,128)(2,1)S(1)}, bf16[2,18,42,384]{3,2,0,1:T(8,128)(2,1)}, bf16[2,18,42,384]{3,2,0,1:T(8,128)(2,1)S(1)}) fusion(bf16[4,16,40,384]{3,2,0,1:T(8,128)(2,1)S(1)} %bitcast.211), kind=kLoop, calls=%fused_computation.2 | loop fusion | bytes 5449728 | tf_op jit(solution)/shard_map/slice | solution.py:32
  172.0 1.3 reshape.174
  173.4 1.9 fusion.41
  175.3 4.3 %reshape.176 = f32[2,18,42,3,3,24]{2,1,0,5,4,3:T(8,128)} reshape(f32[1512,216]{0,1:T(8,128)S(1)} %fusion.41) | data formatting | bytes 2612736 | tf_op jit(solution)/shard_map/reshape | solution.py:41
  179.6 1.5 copy.63
  181.1 1.4 reshape.171
  182.4 1.9 fusion.40
  184.3 4.4 %reshape.173 = f32[2,18,42,3,3,24]{2,1,0,5,4,3:T(8,128)} reshape(f32[1512,216]{0,1:T(8,128)S(1)} %fusion.40) | data formatting | bytes 2612736 | tf_op jit(solution)/shard_map/reshape | solution.py:41
  188.8 0.3 reshape.168
  189.2 0.6 fusion.39
  189.8 4.3 %reshape.170 = f32[2,18,42,3,3,24]{2,1,0,5,4,3:T(8,128)} reshape(f32[1512,216]{0,1:T(8,128)S(1)} %fusion.39) | data formatting | bytes 2612736 | tf_op jit(solution)/shard_map/reshape | solution.py:41
  194.1 7.0 %fusion.1 = f32[2,16,40,24]{2,1,0,3:T(8,128)S(1)} fusion(f32[2,18,42,3,3,24]{2,1,0,5,4,3:T(8,128)} %reshape.176, f32[2,18,42,3,3,24]{2,1,0,5,4,3:T(8,128)} %reshape.173, f32[2,18,42,3,3,24]{2,1,0,5,4,3:T(8,128)} %reshape.170, f32[24]{0:T(128)S(1)} %dynamic_slice.7), kind=kLoop, calls=%fused_computation.8 | loop fusion | flops 829440 | bytes 3440736 | tf_op jit(solution)/shard_map/add | solution.py:50
  201.3 0.7 reshape.205
  202.0 13.6 %all_to_all.33 = f32[16,1,1920]{2,1,0:T(1,128)S(1)} all-to-all(f32[16,1,1920]{2,1,0:T(1,128)S(1)} %reshape.205), channel_id=1, replica_groups=mesh['tm'=32,'rows'=16] {'rows'}, dimensions={0} | all-to-all | bytes 245760 | tf_op jit(solution)/shard_map/all_to_all | solution.py:71
  215.6 0.5 broadcast.96
  216.1 0.9 reduce.5
  217.0 0.7 reshape.206
  217.9 0.6 fusion.33
  (26 shorter events, 1.7 us)
Async XLA Ops:
  6.5 58.7 %all-gather.2.cloned.1.call-start = ((), (), s32[]{:S(2)}) async-start(), calls=%async_computation.3 | async-start | bytes 2088960 | tf_op jit(solution)/shard_map/all_gather | solution.py:61
  8.4 5.2 %collective-permute-start = (bf16[2,1,40,384]{3,2,1,0:T(8,128)(2,1)S(1)}, bf16[2,1,40,384]{3,2,1,0:T(8,128)(2,1)S(1)}, u32[]{:S(2)}, u32[]{:S(2)}) collective-permute-start(bf16[2,1,40,384]{3,2,1,0:T(8,128)(2,1)S(1)} %fusion.32), channel_id=1, source_target_pairs={{0,16},{16,32},{32,48},{48,64},{64,80},{80,96},{96,112},{112,128},... | collective-permute-start | bytes 184328 | tf_op jit(solution)/shard_map/ppermute | solution.py:11
  99.2 13.4 %copy-start.4 = (f32[384]{0:T(512)S(1)}, f32[384]{0:T(512)}, u32[]{:S(2)}) copy-start(f32[384]{0:T(512)} %param.11) | copy-start | bytes 4612
  112.7 4.4 %collective-permute-start.1 = (bf16[2,1,40,384]{3,2,1,0:T(8,128)(2,1)S(1)}, bf16[2,1,40,384]{3,2,1,0:T(8,128)(2,1)S(1)}, u32[]{:S(2)}, u32[]{:S(2)}) collective-permute-start(bf16[2,1,40,384]{3,2,1,0:T(8,128)(2,1)S(1)} %multiply_convert_fusion), channel_id=1, source_target_pairs={{0,16},{16,32},{32,48},{48,64},{64,80},{80,96},{96,112},{112,128},... | collective-permute-start | bytes 184328 | tf_op jit(solution)/shard_map/ppermute | solution.py:11
  118.6 5.4 %copy-start.3 = (bf16[24,3,3,3,384]{4,0,3,2,1:T(8,128)(2,1)S(1)}, bf16[24,3,3,3,384]{4,0,3,2,1:T(8,128)(2,1)}, u32[]{:S(2)}) copy-start(bf16[24,3,3,3,384]{4,0,3,2,1:T(8,128)(2,1)} %param.12) | copy-start | bytes 1492996
  118.6 51.0 %all-to-all-start.1 = ((bf16[16,4,1,40,384]{4,3,1,2,0:T(8,128)(2,1)}), bf16[16,4,1,40,384]{4,3,1,2,0:T(8,128)(2,1)S(1)}, u32[]{:S(2)}, u32[]{:S(2)}) async-start(bf16[16,4,1,40,384]{4,3,1,2,0:T(8,128)(2,1)} %stack.2), calls=%async_computation.1 | async-start | bytes 3932160 | tf_op jit(solution)/shard_map/all_to_all | solution.py:68
  172.0 1.3 copy-start.1
  181.1 1.4 copy-start
  201.1 16.8 %copy-start.2 = (bf16[2,1,40,384]{3,2,1,0:T(8,128)(2,1)S(1)}, bf16[2,1,40,384]{3,2,1,0:T(8,128)(2,1)}, u32[]{:S(2)}) copy-start(bf16[2,1,40,384]{3,2,1,0:T(8,128)(2,1)} %param.7) | copy-start | bytes 184324
Sparse Core Ops, SparseCore 0:
  14.5 50.7 all-gather.1
